TPU v7x, 128 devices: a whole 4x4x4 slice. The times are simulated.
128 devices in a mesh: dp: 8 (over z, core), ts: 16 (over y, x).
Axes of the slice: x: 4, y: 4, z: 4, core: 2. Of those that a mesh axis runs over, the one named last changes fastest.
Arguments:
- text_embed: bfloat16 [8, 1024, 4096], P('dp', None, 'ts'), may hold values from -6 to 6
- bridge: bfloat16 [128, 32, 4096], P('dp', None, 'ts'), may hold values from -6 to 6
- crystal_slot: int32 [128], P('dp'), may hold values from 0 to 8159, as said below
- segments: int32 [8, 1024], P('dp'), may hold values from 0 to 15, as said below
- attn_gain: float32 [4096], replicated, may hold values from 0.1 to 1.9
- w_query: bfloat16 [4096, 4096], P(None, 'ts'), as said below
- w_key: bfloat16 [4096, 1024], P(None, 'ts'), may hold values from -0.09375 to 0.09375
- w_value: bfloat16 [4096, 1024], P(None, 'ts'), may hold values from -0.09375 to 0.09375
- w_out: bfloat16 [4096, 4096], P('ts'), may hold values from -0.09375 to 0.09375
- mlp_gain: float32 [4096], replicated, may hold values from 0.1 to 1.9
- w_gate: bfloat16 [4096, 12288], P(None, 'ts'), may hold values from -0.09375 to 0.09375
- w_up: bfloat16 [4096, 12288], P(None, 'ts'), may hold values from -0.09375 to 0.09375
- w_down: bfloat16 [12288, 4096], P('ts'), may hold values from -0.0546875 to 0.0546875
Outputs:
- layer_out: bfloat16 [8, 1024, 4096], P('dp', 'ts')
Inputs may be any that keep to these rules, and one draw needn't show every extreme that they name: `segments`: each row starts at 0, never falls and names every document number of 0 to 15; every document holds at least 33 positions. `crystal_slot`: each crystal's 32 rows take the first 32 positions of one document, given as sequence * 1024 + that document's first position; every document takes exactly one crystal, and each sequence takes exactly 2 of the 16 crystals held by each index of dp. `w_query`: entries lie within plus or minus 104 / sqrt(4096).
All inputs are finite; a program needn't handle non-finite values.
Results may differ from a plain program's by a relative error of at most 0.025.
The roundings to bfloat16 on the way count: a program that leaves them out, or rounds other values in their place, can miss the bound.
Values may be sent and summed in bfloat16 or wider, within the bound.
No kernel may reach another device: no remote copies, remote signals or barrier semaphores. Data moves between devices by JAX's collectives and lax.ppermute only.
A program may use at most 128 MiB of HBM per device.

v0:
```python
import jax
import jax.numpy as jnp
from jax import lax
from jax.sharding import PartitionSpec as P

HD = 128
DOC_LEN = 64
ROW_CHUNKS = 2
COL_CHUNKS = 2
norm_epsilon = 1e-05
rope_base = 500000.0
masked_score = -1e30


def partner_2(block, axis, apart):
    count = lax.axis_size(axis)
    route = []
    for low in range(count):
        high = low | 1 << apart
        if high != low and high < count:
            route += [(low, high), (high, low)]
    return lax.ppermute(block, axis, route)


def norm_rows(rows, gain):
    widened = rows.astype(jnp.float32)
    inverse_rms = lax.rsqrt(jnp.mean(widened * widened, axis=-1, keepdims=True) + norm_epsilon)
    return (widened * inverse_rms * gain).astype(jnp.bfloat16)


def rotate_pairs(values, positions, first_pair):
    pair_count = values.shape[-1] // 2
    exponent = 2.0 * (first_pair + jnp.arange(pair_count, dtype=jnp.int32)).astype(jnp.float32) / HD
    frequency = rope_base ** (-exponent)
    angles = positions.astype(jnp.float32)[:, None] * frequency[None, :]
    cosine = jnp.cos(angles)[:, None, :]
    sine_part = jnp.sin(angles)[:, None, :]
    paired = values.reshape(values.shape[0], values.shape[1], pair_count, 2)
    even_part = paired[..., 0]
    odd_part = paired[..., 1]
    new_even = even_part * cosine - odd_part * sine_part
    new_odd = even_part * sine_part + odd_part * cosine
    return jnp.stack([new_even, new_odd], axis=-1).reshape(values.shape)


def attend_block(query_block, query_segments, query_index, keys_full, values_full, segment_ids):
    scores = jnp.einsum(
        "qhd,kd->hqk", query_block, keys_full, preferred_element_type=jnp.float32
    ) * HD ** (-0.5)
    key_index = jnp.arange(keys_full.shape[0], dtype=jnp.int32)
    allowed = (query_segments[:, None] == segment_ids[None, :]) & (
        key_index[None, :] <= query_index[:, None]
    )
    scores = jnp.where(allowed[None], scores, masked_score)
    row_top = jnp.max(scores, axis=-1, keepdims=True)
    weights = jnp.exp(scores - row_top)
    probabilities = (weights / jnp.sum(weights, axis=-1, keepdims=True)).astype(jnp.bfloat16)
    mixed_rows = jnp.einsum(
        "hqk,kd->qhd", probabilities, values_full, preferred_element_type=jnp.float32
    )
    return mixed_rows.astype(jnp.bfloat16).reshape(query_block.shape[0], -1)


def after(ready, value):
    return lax.optimization_barrier((ready, value))[1]


def shards(
    text_embed,
    bridge,
    crystal_slot,
    segments,
    attn_gain,
    w_query,
    w_key,
    w_value,
    w_out,
    mlp_gain,
    w_gate,
    w_up,
    w_down,
):
    seq_len = text_embed.shape[1]
    part_width = text_embed.shape[2]
    doc_count = seq_len // DOC_LEN
    bridge_len = bridge.shape[1]
    tok_rows = seq_len // lax.axis_size("ts")
    group_index = lax.axis_index("dp")
    ts_index = lax.axis_index("ts")
    segment_ids = segments[0]
    doc_numbers = jnp.arange(doc_count, dtype=jnp.int32)
    starts = jnp.sum((segment_ids[None, :] < doc_numbers[:, None]).astype(jnp.int32), axis=1)
    doc_match = segment_ids[:, None] == doc_numbers[None, :]
    positions = jnp.arange(seq_len, dtype=jnp.int32) - jnp.sum(
        jnp.where(doc_match, starts[None, :], 0), axis=1
    )
    flat_bridge = bridge.reshape(bridge.shape[0], bridge_len * part_width)
    slot_high = (crystal_slot // 128).astype(jnp.bfloat16)
    slot_low = (crystal_slot % 128).astype(jnp.bfloat16)
    slot_cols = jnp.zeros((bridge.shape[0], 128), jnp.bfloat16)
    slot_cols = slot_cols.at[:, 0].set(slot_high).at[:, 1].set(slot_low)
    arrived_all = lax.all_gather(
        jnp.concatenate([flat_bridge, slot_cols], axis=1), "dp", axis=0, tiled=True
    )
    arrived = arrived_all[:, : bridge_len * part_width]
    arrived_slots = arrived_all[:, -128].astype(jnp.int32) * 128 + arrived_all[:, -127].astype(
        jnp.int32
    )
    wanted = group_index * seq_len + starts
    picking = wanted[:, None] == arrived_slots[None, :]
    by_doc = jnp.dot(
        picking.astype(jnp.bfloat16), arrived, preferred_element_type=jnp.float32
    ).astype(jnp.bfloat16)
    by_doc = by_doc.reshape(doc_count * bridge_len, part_width)
    in_bridge = positions < bridge_len
    row_pick = (segment_ids * bridge_len + positions)[:, None] == jnp.arange(
        doc_count * bridge_len, dtype=jnp.int32
    )[None, :]
    row_pick = row_pick & in_bridge[:, None]
    filled = jnp.dot(
        row_pick.astype(jnp.bfloat16), by_doc, preferred_element_type=jnp.float32
    ).astype(jnp.bfloat16)
    own_part = jnp.where(in_bridge[:, None], filled, text_embed[0])
    chunk_rows = seq_len // ROW_CHUNKS
    heads_here = w_query.shape[1] // HD
    kv_cols = w_key.shape[1]
    upper_half = ts_index % 2 == 1
    packed_chunks = []
    keys_chunks = []
    values_chunks = []
    after_chunks = []
    hidden_chunks = []
    previous = None
    previous_sum = None
    gate = None
    for chunk in range(ROW_CHUNKS):
        rows = slice(chunk * chunk_rows, (chunk + 1) * chunk_rows)
        local_rows = own_part[rows]
        if previous is not None:
            local_rows = after(previous, local_rows)
        packed = lax.all_gather(local_rows, "ts", axis=1, tiled=True)
        previous = packed
        if gate is not None:
            packed = after(gate, packed)
        packed_chunks.append(packed)
        chunk_positions = positions[rows]
        normed = norm_rows(packed, attn_gain)
        queries = jnp.dot(normed, w_query, preferred_element_type=jnp.float32).reshape(
            chunk_rows, heads_here, HD
        )
        queries = rotate_pairs(queries, chunk_positions, 0).astype(jnp.bfloat16)
        key_half = jnp.dot(normed, w_key, preferred_element_type=jnp.float32).reshape(
            chunk_rows, 1, kv_cols
        )
        key_half = rotate_pairs(key_half, chunk_positions, ts_index % 2 * (kv_cols // 2))
        key_half = key_half.astype(jnp.bfloat16).reshape(chunk_rows, kv_cols)
        value_half = jnp.dot(normed, w_value, preferred_element_type=jnp.float32).astype(
            jnp.bfloat16
        )
        own_pair = jnp.concatenate([key_half, value_half], axis=1)
        partner = partner_2(own_pair, "ts", 0)
        lower_half = jnp.where(upper_half, partner, own_pair)
        higher = jnp.where(upper_half, own_pair, partner)
        keys_chunks.append(jnp.concatenate([lower_half[:, :kv_cols], higher[:, :kv_cols]], axis=1))
        values_chunks.append(
            jnp.concatenate([lower_half[:, kv_cols:], higher[:, kv_cols:]], axis=1)
        )
        keys_seen = jnp.concatenate(keys_chunks, axis=0)
        values_seen = jnp.concatenate(values_chunks, axis=0)
        end_row = (chunk + 1) * chunk_rows
        query_index = jnp.arange(chunk * chunk_rows, end_row, dtype=jnp.int32)
        attended = attend_block(
            queries, segment_ids[rows], query_index, keys_seen, values_seen, segment_ids[:end_row]
        )
        gate = attended
        partial_rows = jnp.dot(attended, w_out, preferred_element_type=jnp.float32).astype(
            jnp.bfloat16
        )
        if previous_sum is not None:
            partial_rows = after(previous_sum, partial_rows)
        attn_sum = lax.psum(partial_rows, "ts")
        previous_sum = attn_sum
        after_attn = (packed.astype(jnp.float32) + attn_sum.astype(jnp.float32)).astype(
            jnp.bfloat16
        )
        after_chunks.append(after_attn)
        normed_mlp = norm_rows(after_attn, mlp_gain)
        gate_proj = jnp.dot(normed_mlp, w_gate, preferred_element_type=jnp.float32)
        up_proj = jnp.dot(normed_mlp, w_up, preferred_element_type=jnp.float32)
        hidden_chunks.append((jax.nn.silu(gate_proj) * up_proj).astype(jnp.bfloat16))
    hidden = jnp.concatenate(hidden_chunks, axis=0)
    after_all = jnp.concatenate(after_chunks, axis=0)
    after_mine = lax.dynamic_slice_in_dim(after_all, ts_index * tok_rows, tok_rows, 0)
    out_cols = w_down.shape[1] // COL_CHUNKS
    mlp_parts = []
    previous_part = None
    for col in range(COL_CHUNKS):
        down = jnp.dot(
            hidden,
            w_down[:, col * out_cols : (col + 1) * out_cols],
            preferred_element_type=jnp.float32,
        ).astype(jnp.bfloat16)
        if previous_part is not None:
            down = after(previous_part, down)
        part = lax.psum_scatter(down, "ts", scatter_dimension=0, tiled=True)
        previous_part = part
        mlp_parts.append(part)
    mlp_mine = jnp.concatenate(mlp_parts, axis=1).astype(jnp.float32)
    layer_rows = (after_mine.astype(jnp.float32) + mlp_mine).astype(jnp.bfloat16)
    return layer_rows.reshape(1, tok_rows, layer_rows.shape[1])


def solution(mesh):
    return jax.shard_map(
        shards,
        mesh=mesh,
        in_specs=(
            P("dp", None, "ts"),
            P("dp", None, "ts"),
            P("dp"),
            P("dp", None),
            P(),
            P(None, "ts"),
            P(None, "ts"),
            P(None, "ts"),
            P("ts", None),
            P(),
            P(None, "ts"),
            P(None, "ts"),
            P("ts", None),
        ),
        out_specs=P("dp", "ts", None),
        check_vma=False,
    )
```

profile of v0, /device:TPU:0, one launch (start us, length us, event | category | flops | bytes accessed | tf_op | source)
XLA Modules:
  0.0 565.7 jit_solution(9591049494155157957)
XLA Ops:
  14.0 25.7 %all-gather.4.cloned.1.call-done = bf16[128,8320]{1,0:T(8,128)(2,1)} async-done(((bf16[16,8320]{1,0:T(8,128)(2,1)}), bf16[128,8320]{1,0:T(8,128)(2,1)}) %all-gather.4.cloned.1.call-update) | async-done | bytes 2129936 | tf_op jit(solution)/shard_map/all_gather | solution.py:102
  40.8 2.0 convolution_convert_fusion
  44.9 57.9 %all-gather.6.cloned.1.call-done = bf16[512,4096]{1,0:T(8,128)(2,1)} async-done(((bf16[512,256]{1,0:T(8,128)(2,1)}), bf16[512,4096]{1,0:T(8,128)(2,1)}) %all-gather.6.cloned.1.call-update) | async-done | bytes 4194320 | tf_op jit(solution)/shard_map/all_gather | solution.py:141
  107.5 3.1 fusion.8
  112.3 2.0 copy-done.6
  117.1 3.7 convolution_convert_fusion.7
  123.1 3.8 fusion.133
  126.9 2.1 reshape_reshape.13
  134.8 4.0 fusion.124
  138.8 2.0 convolution_convert_fusion.5
  140.8 3.2 convolution_convert_fusion.2
  144.1 17.8 %all-gather.8.cloned.1.call-done = bf16[512,4096]{1,0:T(8,128)(2,1)} async-done(((bf16[512,256]{1,0:T(8,128)(2,1)}), bf16[512,4096]{1,0:T(8,128)(2,1)}) %all-gather.8.cloned.1.call-update) | async-done | bytes 4194320 | tf_op jit(solution)/shard_map/all_gather | solution.py:141
  161.9 3.2 fusion.12
  167.0 2.0 copy-done.4
  171.0 4.4 convolution_convert_fusion.6
  177.1 3.7 fusion.135
  185.9 4.6 fusion.127
  190.5 2.7 fusion.41
  193.2 3.3 convolution_convert_fusion.1
  196.5 74.1 %all-reduce.4.cloned.1.call-done = bf16[512,4096]{1,0:T(8,128)(2,1)} async-done(((bf16[512,4096]{1,0:T(8,128)(2,1)}), bf16[512,4096]{1,0:T(8,128)(2,1)}) %all-reduce.4.cloned.1.call-update) | async-done | bytes 4194320 | tf_op jit(solution)/shard_map/psum | solution.py:181
  270.7 5.6 fusion.2
  276.3 7.5 %fusion.39 = f32[512,768]{1,0:T(8,128)S(1)} fusion(bf16[4096,768]{1,0:T(8,128)(2,1)} %param.27, bf16[512,4096]{1,0:T(8,128)(2,1)S(1)} %get-tuple-element.38, f32[4096]{0:T(1024)S(1)} %copy-done.27, f32[512]{0:T(512)S(1)} %add_rsqrt_fusion.1), kind=kOutput, calls=%fused_computation.59 | convolution fusion | flops 3229614080 | bytes 12077056 | tf_op jit(solution)/shard_map/dot_general | solution.py:188
  283.8 3.6 multiply_convert_fusion.1
  287.4 89.4 %all-reduce.6.cloned.1.call-done = bf16[512,4096]{1,0:T(8,128)(2,1)} async-done(((bf16[512,4096]{1,0:T(8,128)(2,1)}), bf16[512,4096]{1,0:T(8,128)(2,1)}) %all-reduce.6.cloned.1.call-update) | async-done | bytes 4194320 | tf_op jit(solution)/shard_map/psum | solution.py:181
  376.9 5.6 fusion.5
  382.5 7.2 %fusion.36 = f32[512,768]{1,0:T(8,128)S(1)} fusion(bf16[4096,768]{1,0:T(8,128)(2,1)} %param.27, bf16[512,4096]{1,0:T(8,128)(2,1)S(1)} %get-tuple-element.40, f32[512]{0:T(512)S(1)} %add_rsqrt_fusion, f32[4096]{0:T(1024)S(1)} %copy-done.27), kind=kOutput, calls=%fused_computation.58 | convolution fusion | flops 3229614080 | bytes 12077056 | tf_op jit(solution)/shard_map/dot_general | solution.py:188
  389.8 3.6 multiply_convert_fusion
  393.4 5.0 convolution_convert_fusion.4
  398.5 7.7 %convolution_convert_fusion.3 = bf16[1024,2048]{1,0:T(8,128)(2,1)} fusion(bf16[768,4096]{1,0:T(8,128)(2,1)} %param.29, bf16[512,768]{1,0:T(8,128)(2,1)S(1)} %multiply_convert_fusion, bf16[512,768]{1,0:T(8,128)(2,1)S(1)} %multiply_convert_fusion.1), kind=kOutput, calls=%fused_computation.34 | convolution fusion | flops 3226468352 | bytes 8912896 | tf_op jit(solution)/shard_map/dot_general | solution.py:198
  406.1 69.7 %reduce-scatter.3.cloned.1.call-done = bf16[64,2048]{1,0:T(8,128)(2,1)} async-done(((bf16[1024,2048]{1,0:T(8,128)(2,1)}), bf16[64,2048]{1,0:T(8,128)(2,1)}) %reduce-scatter.3.cloned.1.call-update) | async-done | bytes 262160 | tf_op jit(solution)/shard_map/reduce_scatter | solution.py:205
  475.9 80.6 %reduce-scatter.5.cloned.1.call-done = bf16[64,2048]{1,0:T(8,128)(2,1)} async-done(((bf16[1024,2048]{1,0:T(8,128)(2,1)}), bf16[64,2048]{1,0:T(8,128)(2,1)}) %reduce-scatter.5.cloned.1.call-update) | async-done | bytes 262160 | tf_op jit(solution)/shard_map/reduce_scatter | solution.py:205
  556.5 2.2 fusion.49
  (146 shorter events, 38.4 us)
Async XLA Ops:
  6.5 134.3 %copy-start = (bf16[256,4096]{1,0:T(8,128)(2,1)S(1)}, bf16[256,4096]{1,0:T(8,128)(2,1)}, u32[]{:S(2)}) copy-start(bf16[256,4096]{1,0:T(8,128)(2,1)} %param.25) | copy-start | bytes 6291460
  6.5 36.4 %copy-start.26 = (bf16[1,1024,256]{2,1,0:T(8,128)(2,1)S(1)}, bf16[1,1024,256]{2,1,0:T(8,128)(2,1)}, u32[]{:S(2)}) copy-start(bf16[1,1024,256]{2,1,0:T(8,128)(2,1)} %param.17) | copy-start | bytes 1572868
  6.5 33.2 %all-gather.4.cloned.1.call-start = ((), (), s32[]{:S(2)}) async-start(), calls=%async_computation.2 | async-start | bytes 2396160 | tf_op jit(solution)/shard_map/all_gather | solution.py:102
  10.9 92.6 %copy-start.16 = (s32[1,1024]{1,0:T(1,128)S(1)}, s32[1,1024]{1,0:T(1,128)}, u32[]{:S(2)}) copy-start(s32[1,1024]{1,0:T(1,128)} %param.20) | copy-start | bytes 12292
  11.7 91.2 %all-gather.6.cloned.1.call-start = ((), (), s32[]{:S(2)}) async-start(), calls=%async_computation.3 | async-start | bytes 4456448 | tf_op jit(solution)/shard_map/all_gather | solution.py:141
  44.0 66.6 %copy-start.17 = (f32[4096]{0:T(1024)S(1)}, f32[4096]{0:T(1024)}, u32[]{:S(2)}) copy-start(f32[4096]{0:T(1024)} %param.21) | copy-start | bytes 49156
  44.9 117.0 %all-gather.8.cloned.1.call-start = ((), (), s32[]{:S(2)}) async-start(), calls=%async_computation.5 | async-start | bytes 4456448 | tf_op jit(solution)/shard_map/all_gather | solution.py:141
  102.9 167.7 %all-reduce.4.cloned.1.call-start = ((), (), s32[]{:S(2)}) async-start(), calls=%async_computation.4 | async-start | bytes 8388608 | tf_op jit(solution)/shard_map/psum | solution.py:181
  102.9 7.7 %copy-start.3 = (bf16[512,4096]{1,0:T(8,128)(2,1)S(1)}, bf16[512,4096]{1,0:T(8,128)(2,1)}, u32[]{:S(2)}) copy-start(bf16[512,4096]{1,0:T(8,128)(2,1)} %all-gather.6.cloned.1.call-done) | copy-start | bytes 12582916
  103.6 7.0 %copy-start.22 = (f32[512]{0:T(512)}, f32[512]{0:T(512)S(1)}, u32[]{:S(2)}) copy-start(f32[512]{0:T(512)S(1)} %get-tuple-element.71) | copy-start | bytes 6148
  103.6 7.0 %copy-start.24 = (f32[512]{0:T(512)}, f32[512]{0:T(512)S(1)}, u32[]{:S(2)}) copy-start(f32[512]{0:T(512)S(1)} %get-tuple-element.72) | copy-start | bytes 6148
  117.1 6.0 %copy-start.7 = (bf16[512,4096]{1,0:T(8,128)(2,1)S(1)}, bf16[512,4096]{1,0:T(8,128)(2,1)}, u32[]{:S(2)}) copy-start(bf16[512,4096]{1,0:T(8,128)(2,1)} %copy-done.6) | copy-start | bytes 12582916
  121.5 9.2 %copy-start.14 = (f32[512,64]{0,1:T(8,128)S(1)}, f32[512,64]{0,1:T(8,128)}, u32[]{:S(2)}) copy-start(f32[512,64]{0,1:T(8,128)} %get-tuple-element.81) | copy-start | bytes 393220
  121.5 11.7 %collective-permute-start = (bf16[512,128]{0,1:T(8,128)(2,1)}, bf16[512,128]{0,1:T(8,128)(2,1)}, u32[]{:S(2)}, u32[]{:S(2)}) collective-permute-start(bf16[512,128]{0,1:T(8,128)(2,1)} %pad_maximum_fusion.6), channel_id=1, source_target_pairs={{0,1},{1,0},{2,3},{3,2},{4,5},{5,4},{6,7},{7,6},{8,9},{9,8},{10,11... | collective-permute-start | bytes 393224 | tf_op jit(solution)/shard_map/ppermute | solution.py:22
  144.0 232.8 %all-reduce.6.cloned.1.call-start = ((), (), s32[]{:S(2)}) async-start(), calls=%async_computation.6 | async-start | bytes 8388608 | tf_op jit(solution)/shard_map/psum | solution.py:181
  171.0 6.0 %copy-start.5 = (bf16[512,4096]{1,0:T(8,128)(2,1)S(1)}, bf16[512,4096]{1,0:T(8,128)(2,1)}, u32[]{:S(2)}) copy-start(bf16[512,4096]{1,0:T(8,128)(2,1)} %copy-done.4) | copy-start | bytes 12582916
  176.1 6.5 %copy-start.13 = (f32[512,64]{0,1:T(8,128)S(1)}, f32[512,64]{0,1:T(8,128)}, u32[]{:S(2)}) copy-start(f32[512,64]{0,1:T(8,128)} %get-tuple-element.78) | copy-start | bytes 393220
  176.1 8.7 %collective-permute-start.1 = (bf16[512,128]{0,1:T(8,128)(2,1)}, bf16[512,128]{0,1:T(8,128)(2,1)}, u32[]{:S(2)}, u32[]{:S(2)}) collective-permute-start(bf16[512,128]{0,1:T(8,128)(2,1)} %pad_maximum_fusion.7), channel_id=1, source_target_pairs={{0,1},{1,0},{2,3},{3,2},{4,5},{5,4},{6,7},{7,6},{8,9},{9,8},{10,11... | collective-permute-start | bytes 393224 | tf_op jit(solution)/shard_map/ppermute | solution.py:22
  180.8 5.1 copy-start.12
  185.8 4.6 copy-start.18
  270.6 5.7 %copy-start.27 = (f32[4096]{0:T(1024)S(1)}, f32[4096]{0:T(1024)}, u32[]{:S(2)}) copy-start(f32[4096]{0:T(1024)} %param.26) | copy-start | bytes 49156
  270.6 205.3 %reduce-scatter.3.cloned.1.call-start = ((), (), s32[]{:S(2)}) async-start(), calls=%async_computation.7 | async-start | bytes 4456448 | tf_op jit(solution)/shard_map/reduce_scatter | solution.py:205
  270.6 13.1 %slice-start = ((s8[6291456]{0:T(1024)(128)(4,1)}), s8[4194304]{0:T(1024)(128)(4,1)S(1)}, s32[]{:S(2)}) async-start(s8[6291456]{0:T(1024)(128)(4,1)} %bitcast.109), calls=%async_computation.9 | async-start | bytes 8388608
  276.2 7.5 %copy-start.8 = (bf16[512,4096]{1,0:T(8,128)(2,1)}, bf16[512,4096]{1,0:T(8,128)(2,1)S(1)}, u32[]{:S(2)}) copy-start(bf16[512,4096]{1,0:T(8,128)(2,1)S(1)} %get-tuple-element.38) | copy-start | bytes 12582916
  276.3 7.5 %slice-start.1 = ((s8[6291456]{0:T(1024)(128)(4,1)}), s8[2097152]{0:T(1024)(128)(4,1)S(1)}, s32[]{:S(2)}) async-start(s8[6291456]{0:T(1024)(128)(4,1)} %bitcast.109), calls=%async_computation.10 | async-start | bytes 4194304
  376.9 12.9 %slice-start.2 = ((s8[6291456]{0:T(1024)(128)(4,1)}), s8[4194304]{0:T(1024)(128)(4,1)S(1)}, s32[]{:S(2)}) async-start(s8[6291456]{0:T(1024)(128)(4,1)} %bitcast.111), calls=%async_computation.11 | async-start | bytes 8388608
  382.4 7.3 %copy-start.9 = (bf16[512,4096]{1,0:T(8,128)(2,1)}, bf16[512,4096]{1,0:T(8,128)(2,1)S(1)}, u32[]{:S(2)}) copy-start(bf16[512,4096]{1,0:T(8,128)(2,1)S(1)} %get-tuple-element.40) | copy-start | bytes 12582916
  382.5 7.2 %slice-start.3 = ((s8[6291456]{0:T(1024)(128)(4,1)}), s8[2097152]{0:T(1024)(128)(4,1)S(1)}, s32[]{:S(2)}) async-start(s8[6291456]{0:T(1024)(128)(4,1)} %bitcast.111), calls=%async_computation.12 | async-start | bytes 4194304
  382.5 10.9 %slice-start.4 = ((s8[6291456]{0:T(1024)(128)(4,1)}), s8[4194304]{0:T(1024)(128)(4,1)S(1)}, s32[]{:S(2)}) async-start(s8[6291456]{0:T(1024)(128)(4,1)} %bitcast.113), calls=%async_computation.13 | async-start | bytes 8388608
  398.4 158.1 %reduce-scatter.5.cloned.1.call-start = ((), (), s32[]{:S(2)}) async-start(), calls=%async_computation.8 | async-start | bytes 4456448 | tf_op jit(solution)/shard_map/reduce_scatter | solution.py:205
  475.9 80.6 %copy-start.15 = (bf16[64,2048]{1,0:T(8,128)(2,1)S(1)}, bf16[64,2048]{1,0:T(8,128)(2,1)}, u32[]{:S(2)}) copy-start(bf16[64,2048]{1,0:T(8,128)(2,1)} %reduce-scatter.3.cloned.1.call-done) | copy-start | bytes 786436
  475.9 82.8 %copy-start.1 = (bf16[256,4096]{1,0:T(8,128)(2,1)S(1)}, bf16[256,4096]{1,0:T(8,128)(2,1)}, u32[]{:S(2)}) copy-start(bf16[256,4096]{1,0:T(8,128)(2,1)} %param.25) | copy-start | bytes 6291460
  (11 other events, 33.3 us)
Sparse Core Ops, SparseCore 0:
  11.8 27.8 all-gather.3
  45.0 57.8 all-gather.5
  105.0 56.8 all-gather.7
  165.1 105.4 all-reduce.3
  273.8 103.0 all-reduce.5
  398.5 77.2 reduce-scatter.2
  479.6 76.8 reduce-scatter.4
where the time goes:
time: 573 us; the launch traced here: 566 us
  waiting for transfers between devices  417 us (73%)
  matrix products  75.9 us (13%)
  other arithmetic  42.6 us (7%)
  between operations  14.4 us (3%)
  local copies, waits for them, and re-layouts  13.4 us (2%)
    psum x2, waiting for transfers between devices, shards(): attn_sum = lax.psum(partial_rows, 'ts')  164 us
    reduce_scatter x2, waiting for transfers between devices, shards(): part = lax.psum_scatter(down, 'ts', scatter_dimension=0, tiled=True)  150 us
    all_gather x2, waiting for transfers between devices, shards(): packed = lax.all_gather(local_rows, 'ts', axis=1, tiled=True)  75.7 us
    all_gather x1, waiting for transfers between devices, shards(): lax.all_gather(jnp.concatenate([flat_bridge, slot_cols], axis=1), 'dp', a...  25.7 us
    reduce_sum x4, other arithmetic, norm_rows(): jnp.mean(widened * widened, axis=-1, keepdims=True) + norm_epsilon  17.5 us
    dot_general x2, matrix products, shards(): gate_proj = jnp.dot(normed_mlp, w_gate, preferred_element_type=jnp.float32)  14.7 us
    dot_general x2, matrix products, shards(): jnp.dot(hidden, w_down[:, col * out_cols:(col + 1) * out_cols], preferred...  12.6 us
  transfers between devices with their start and end apart: 9, of which 8 were waited for; matrix products, arithmetic and copies ran while one was open for 17% of the time, Pallas kernels for 0%

commit v1 on v0

--- a/solution.py
+++ b/solution.py
@@ -178,7 +178,7 @@
         )
         if previous_sum is not None:
             partial_rows = after(previous_sum, partial_rows)
-        attn_sum = lax.psum(partial_rows, "ts")
+        attn_sum = jnp.sum(lax.all_gather(partial_rows, "ts"), axis=0)
         previous_sum = attn_sum
         after_attn = (packed.astype(jnp.float32) + attn_sum.astype(jnp.float32)).astype(
             jnp.bfloat16

time: 573 us -> 1140 us (1.99)
  waiting for transfers between devices: 417 us -> 940 us
  other arithmetic: 42.6 us -> 90.2 us
    all_gather x0 -> x2, waiting for transfers between devices: none -> 687 us  [shards(): attn_sum = jnp.sum(lax.all_gather(partial_rows, 'ts'), axis=0)]
    psum x2 -> x0, waiting for transfers between devices: 164 us -> none  [shards(): attn_sum = lax.psum(partial_rows, 'ts')]
    reduce_sum x0 -> x2, other arithmetic: none -> 47.4 us  [shards(): attn_sum = jnp.sum(lax.all_gather(partial_rows, 'ts'), axis=0)]
  transfers between devices with their start and end apart: 9 -> 9, of which waited for: 8 -> 8; matrix products, arithmetic and copies ran while one was open for 17% -> 8% of each run, Pallas kernels for 0% -> 0%
where the time goes in v1:
time: 1140 us
  waiting for transfers between devices  940 us (82%)
  other arithmetic  90.2 us (8%)
  matrix products  76.2 us (7%)
  between operations  14.4 us (1%)
  local copies, waits for them, and re-layouts  13.4 us (1%)
    all_gather x2, waiting for transfers between devices, shards(): attn_sum = jnp.sum(lax.all_gather(partial_rows, 'ts'), axis=0)  687 us
    reduce_scatter x2, waiting for transfers between devices, shards(): part = lax.psum_scatter(down, 'ts', scatter_dimension=0, tiled=True)  150 us
    all_gather x2, waiting for transfers between devices, shards(): packed = lax.all_gather(local_rows, 'ts', axis=1, tiled=True)  76.9 us
    reduce_sum x2, other arithmetic, shards(): attn_sum = jnp.sum(lax.all_gather(partial_rows, 'ts'), axis=0)  47.4 us
    all_gather x1, waiting for transfers between devices, shards(): lax.all_gather(jnp.concatenate([flat_bridge, slot_cols], axis=1), 'dp', a...  25.7 us
  transfers between devices with their start and end apart: 9, of which 8 were waited for; matrix products, arithmetic and copies ran while one was open for 8% of the time, Pallas kernels for 0%

profile of v1, /device:TPU:0, one launch (start us, length us, event | category | flops | bytes accessed | tf_op | source)
XLA Modules:
  0.0 1137.0 jit_solution(1720552616174948454)
XLA Ops:
  14.2 25.7 %all-gather.8.cloned.1.call-done = bf16[128,8320]{1,0:T(8,128)(2,1)} async-done(((bf16[16,8320]{1,0:T(8,128)(2,1)}), bf16[128,8320]{1,0:T(8,128)(2,1)}) %all-gather.8.cloned.1.call-update) | async-done | bytes 2129936 | tf_op jit(solution)/shard_map/all_gather | solution.py:102
  40.9 2.0 convolution_convert_fusion
  45.1 57.9 %all-gather.10.cloned.1.call-done = bf16[512,4096]{1,0:T(8,128)(2,1)} async-done(((bf16[512,256]{1,0:T(8,128)(2,1)}), bf16[512,4096]{1,0:T(8,128)(2,1)}) %all-gather.10.cloned.1.call-update) | async-done | bytes 4194320 | tf_op jit(solution)/shard_map/all_gather | solution.py:141
  106.4 3.1 fusion.8
  115.9 3.7 convolution_convert_fusion.7
  121.9 3.7 fusion.133
  125.6 2.1 reshape_reshape.13
  133.5 3.4 fusion.124
  136.9 2.1 convolution_convert_fusion.5
  139.0 3.3 convolution_convert_fusion.2
  143.6 18.9 %all-gather.12.cloned.1.call-done = bf16[512,4096]{1,0:T(8,128)(2,1)} async-done(((bf16[512,256]{1,0:T(8,128)(2,1)}), bf16[512,4096]{1,0:T(8,128)(2,1)}) %all-gather.12.cloned.1.call-update) | async-done | bytes 4194320 | tf_op jit(solution)/shard_map/all_gather | solution.py:141
  162.5 3.2 fusion.12
  171.7 4.5 convolution_convert_fusion.6
  177.9 4.1 fusion.135
  186.0 4.6 fusion.127
  190.7 2.7 fusion.41
  193.4 3.3 convolution_convert_fusion.1
  196.7 335.8 %all-gather.14.cloned.1.call-done = bf16[8192,4096]{1,0:T(8,128)(2,1)} async-done(((bf16[512,4096]{1,0:T(8,128)(2,1)}), bf16[8192,4096]{1,0:T(8,128)(2,1)}) %all-gather.14.cloned.1.call-update) | async-done | bytes 67108880 | tf_op jit(solution)/shard_map/all_gather | solution.py:181
  532.5 23.7 %reduce_sum.100 = bf16[512,4096]{1,0:T(8,128)(2,1)} reduce(bf16[16,512,4096]{2,1,0:T(8,128)(2,1)} %bitcast.11, bf16[]{:T(256)} %constant.137.clone.1), dimensions={0}, to_apply=%region_7.8 | reduce | flops 31457280 | bytes 71303168 | tf_op jit(solution)/shard_map/reduce_sum | solution.py:181
  556.3 5.6 fusion.2
  561.9 7.8 fusion.39
  569.7 3.6 multiply_convert_fusion.1
  573.4 351.2 %all-gather.16.cloned.1.call-done = bf16[8192,4096]{1,0:T(8,128)(2,1)} async-done(((bf16[512,4096]{1,0:T(8,128)(2,1)}), bf16[8192,4096]{1,0:T(8,128)(2,1)}) %all-gather.16.cloned.1.call-update) | async-done | bytes 67108880 | tf_op jit(solution)/shard_map/all_gather | solution.py:181
  924.6 23.7 %reduce_sum.103 = bf16[512,4096]{1,0:T(8,128)(2,1)} reduce(bf16[16,512,4096]{2,1,0:T(8,128)(2,1)} %bitcast.20, bf16[]{:T(256)} %constant.137.clone.1), dimensions={0}, to_apply=%region_11.12 | reduce | flops 31457280 | bytes 71303168 | tf_op jit(solution)/shard_map/reduce_sum | solution.py:181
  948.3 5.6 fusion.5
  953.9 7.2 fusion.36
  961.2 3.6 multiply_convert_fusion
  964.8 5.0 convolution_convert_fusion.4
  969.9 7.7 convolution_convert_fusion.3
  977.6 69.6 %reduce-scatter.3.cloned.1.call-done = bf16[64,2048]{1,0:T(8,128)(2,1)} async-done(((bf16[1024,2048]{1,0:T(8,128)(2,1)}), bf16[64,2048]{1,0:T(8,128)(2,1)}) %reduce-scatter.3.cloned.1.call-update) | async-done | bytes 262160 | tf_op jit(solution)/shard_map/reduce_scatter | solution.py:205
  1047.3 80.5 %reduce-scatter.5.cloned.1.call-done = bf16[64,2048]{1,0:T(8,128)(2,1)} async-done(((bf16[1024,2048]{1,0:T(8,128)(2,1)}), bf16[64,2048]{1,0:T(8,128)(2,1)}) %reduce-scatter.5.cloned.1.call-update) | async-done | bytes 262160 | tf_op jit(solution)/shard_map/reduce_scatter | solution.py:205
  1127.8 2.2 fusion.49
  (144 shorter events, 41.4 us)
Async XLA Ops:
  6.5 132.4 %copy-start = (bf16[256,4096]{1,0:T(8,128)(2,1)S(1)}, bf16[256,4096]{1,0:T(8,128)(2,1)}, u32[]{:S(2)}) copy-start(bf16[256,4096]{1,0:T(8,128)(2,1)} %param.25) | copy-start | bytes 6291460
  6.5 36.6 %copy-start.24 = (bf16[1,1024,256]{2,1,0:T(8,128)(2,1)S(1)}, bf16[1,1024,256]{2,1,0:T(8,128)(2,1)}, u32[]{:S(2)}) copy-start(bf16[1,1024,256]{2,1,0:T(8,128)(2,1)} %param.17) | copy-start | bytes 1572868
  6.5 33.4 %all-gather.8.cloned.1.call-start = ((), (), s32[]{:S(2)}) async-start(), calls=%async_computation.2 | async-start | bytes 2396160 | tf_op jit(solution)/shard_map/all_gather | solution.py:102
  11.1 92.6 %copy-start.16 = (s32[1,1024]{1,0:T(1,128)S(1)}, s32[1,1024]{1,0:T(1,128)}, u32[]{:S(2)}) copy-start(s32[1,1024]{1,0:T(1,128)} %param.20) | copy-start | bytes 12292
  11.8 91.2 %all-gather.10.cloned.1.call-start = ((), (), s32[]{:S(2)}) async-start(), calls=%async_computation.3 | async-start | bytes 4456448 | tf_op jit(solution)/shard_map/all_gather | solution.py:141
  43.1 66.4 %copy-start.17 = (f32[4096]{0:T(1024)S(1)}, f32[4096]{0:T(1024)}, u32[]{:S(2)}) copy-start(f32[4096]{0:T(1024)} %param.21) | copy-start | bytes 49156
  45.1 117.5 %all-gather.12.cloned.1.call-start = ((), (), s32[]{:S(2)}) async-start(), calls=%async_computation.4 | async-start | bytes 4456448 | tf_op jit(solution)/shard_map/all_gather | solution.py:141
  103.1 429.4 %all-gather.14.cloned.1.call-start = ((), (), s32[]{:S(2)}) async-start(), calls=%async_computation.7 | async-start | bytes 71303168 | tf_op jit(solution)/shard_map/all_gather | solution.py:181
  103.1 6.4 copy-start.3
  115.8 6.0 copy-start.7
  120.2 9.1 copy-start.14
  120.2 11.6 %collective-permute-start = (bf16[512,128]{0,1:T(8,128)(2,1)}, bf16[512,128]{0,1:T(8,128)(2,1)}, u32[]{:S(2)}, u32[]{:S(2)}) collective-permute-start(bf16[512,128]{0,1:T(8,128)(2,1)} %pad_maximum_fusion.6), channel_id=1, source_target_pairs={{0,1},{1,0},{2,3},{3,2},{4,5},{5,4},{6,7},{7,6},{8,9},{9,8},{10,11... | collective-permute-start | bytes 393224 | tf_op jit(solution)/shard_map/ppermute | solution.py:22
  142.3 23.5 %copy-start.18 = (f32[4096]{0:T(1024)S(1)}, f32[4096]{0:T(1024)}, u32[]{:S(2)}) copy-start(f32[4096]{0:T(1024)} %param.21) | copy-start | bytes 49156
  142.3 782.3 %all-gather.16.cloned.1.call-start = ((), (), s32[]{:S(2)}) async-start(), calls=%async_computation.8 | async-start | bytes 71303168 | tf_op jit(solution)/shard_map/all_gather | solution.py:181
  171.7 6.2 copy-start.5
  176.9 7.1 copy-start.13
  176.9 8.1 collective-permute-start.1
  182.0 4.0 copy-start.12
  186.0 4.7 copy-start.19
  186.0 4.6 copy-start.20
  556.2 5.7 copy-start.25
  556.2 491.0 %reduce-scatter.3.cloned.1.call-start = ((), (), s32[]{:S(2)}) async-start(), calls=%async_computation.5 | async-start | bytes 4456448 | tf_op jit(solution)/shard_map/reduce_scatter | solution.py:205
  556.3 13.5 %slice-start = ((s8[6291456]{0:T(1024)(128)(4,1)}), s8[4194304]{0:T(1024)(128)(4,1)S(1)}, s32[]{:S(2)}) async-start(s8[6291456]{0:T(1024)(128)(4,1)} %bitcast.111), calls=%async_computation.9 | async-start | bytes 8388608
  561.9 7.8 copy-start.8
  561.9 7.8 slice-start.1
  948.3 12.8 %slice-start.2 = ((s8[6291456]{0:T(1024)(128)(4,1)}), s8[4194304]{0:T(1024)(128)(4,1)S(1)}, s32[]{:S(2)}) async-start(s8[6291456]{0:T(1024)(128)(4,1)} %bitcast.113), calls=%async_computation.11 | async-start | bytes 8388608
  953.9 7.2 copy-start.9
  953.9 7.2 slice-start.3
  953.9 10.9 slice-start.4
  969.8 157.9 %reduce-scatter.5.cloned.1.call-start = ((), (), s32[]{:S(2)}) async-start(), calls=%async_computation.6 | async-start | bytes 4456448 | tf_op jit(solution)/shard_map/reduce_scatter | solution.py:205
  1047.2 80.6 %copy-start.15 = (bf16[64,2048]{1,0:T(8,128)(2,1)S(1)}, bf16[64,2048]{1,0:T(8,128)(2,1)}, u32[]{:S(2)}) copy-start(bf16[64,2048]{1,0:T(8,128)(2,1)} %reduce-scatter.3.cloned.1.call-done) | copy-start | bytes 786436
  1047.3 82.7 %copy-start.1 = (bf16[256,4096]{1,0:T(8,128)(2,1)S(1)}, bf16[256,4096]{1,0:T(8,128)(2,1)}, u32[]{:S(2)}) copy-start(bf16[256,4096]{1,0:T(8,128)(2,1)} %param.25) | copy-start | bytes 6291460
  (9 other events, 25.7 us)
Sparse Core Ops, SparseCore 0:
  12.0 27.8 all-gather.7
  45.2 57.8 all-gather.9
  105.2 57.3 all-gather.11
  164.5 367.8 all-gather.13
  556.3 368.2 all-gather.15
  970.0 77.2 reduce-scatter.2
  1050.9 76.8 reduce-scatter.4
